TPU v7x, 32 devices: a whole 2x2x4 slice. The times are simulated.
32 devices in a mesh: dp: 8 (over y, x, core), tensor: 4 (over z).
Axes of the slice: x: 2, y: 2, z: 4, core: 2. Of those that a mesh axis runs over, the one named last changes fastest.
Arguments:
- grad_out: bfloat16 [2048, 4096], P('dp'), may hold values from -1.5 to 1.5
- gate_input: bfloat16 [2048, 14336], P('dp', 'tensor'), may hold values from -6 to 6
- up_input: bfloat16 [2048, 14336], P('dp', 'tensor'), may hold values from -6 to 6
- next_hidden: bfloat16 [2048, 14336], P('dp', 'tensor'), may hold values from -6 to 6
- down_weight: bfloat16 [4096, 14336], P(None, 'tensor'), may hold values from -0.046875 to 0.046875
- first_moment: float32 [4096, 14336], P('dp', 'tensor'), may hold values from -48 to 48
- second_moment: float32 [4096, 14336], P('dp', 'tensor'), may hold values from 10 to 200
Outputs:
- gate_grad: bfloat16 [2048, 14336], P('dp', 'tensor')
- up_grad: bfloat16 [2048, 14336], P('dp', 'tensor')
- moment_one: float32 [4096, 14336], P('dp', 'tensor')
- moment_two: float32 [4096, 14336], P('dp', 'tensor')
- next_out: bfloat16 [2048, 4096], P('dp', 'tensor')
All inputs are finite; a program needn't handle non-finite values.
Results may differ from a plain program's by a relative error of at most 0.004.
The roundings to bfloat16 on the way count: a program that leaves them out, or rounds other values in their place, can miss the bound.
Values may be sent and summed in bfloat16 or wider, within the bound.
No kernel may reach another device: no remote copies, remote signals or barrier semaphores. Data moves between devices by JAX's collectives and lax.ppermute only.
A program may use at most 256 MiB of HBM per device.

v0:
```python
import jax
import jax.numpy as jnp
from jax import lax
from jax.sharding import PartitionSpec as P

STEP = 20
beta_one = 0.9
beta_two = 0.95
learn_rate = 0.001
decay_rate = 0.1
epsilon = 1e-08


def shards(grad_out, gate_input, up_input, next_hidden, down_weight, first_moment, second_moment):
    n_dp = lax.axis_size("dp")
    n_t = lax.axis_size("tensor")
    me = lax.axis_index("dp")
    col = lax.axis_index("tensor")
    tok = grad_out.shape[0]
    owned_rows = first_moment.shape[0]
    group = n_dp // n_t
    gate_value = gate_input.astype(jnp.float32)
    up_value = up_input.astype(jnp.float32)
    sigmoid_gate = jax.nn.sigmoid(gate_value)
    activated = gate_value * sigmoid_gate
    hidden = (activated * up_value).astype(jnp.bfloat16)
    hidden_all = lax.all_gather(hidden, "dp", axis=0, tiled=True)
    next_all = lax.all_gather(next_hidden, "dp", axis=0, tiled=True)
    grad_rows = lax.all_to_all(grad_out.T, "dp", 0, 1, tiled=True)
    grad_hidden = jnp.dot(grad_out, down_weight, preferred_element_type=jnp.float32)
    gate_grad = (
        grad_hidden * up_value * sigmoid_gate * (1.0 + gate_value * (1.0 - sigmoid_gate))
    ).astype(jnp.bfloat16)
    up_grad = (grad_hidden * activated).astype(jnp.bfloat16)
    weight_grad = jnp.zeros((owned_rows, hidden.shape[1]), jnp.float32)
    for b in range(n_dp):
        block = jnp.dot(
            grad_rows[:, b * tok : (b + 1) * tok],
            hidden_all[b * tok : (b + 1) * tok],
            preferred_element_type=jnp.float32,
        ).astype(jnp.bfloat16)
        weight_grad = weight_grad + block.astype(jnp.float32)
    moment_one = beta_one * first_moment + (1.0 - beta_one) * weight_grad
    moment_two = beta_two * second_moment + (1.0 - beta_two) * weight_grad * weight_grad
    corrected_one = moment_one / (1.0 - beta_one**STEP)
    corrected_two = moment_two / (1.0 - beta_two**STEP)
    old_shard = lax.dynamic_slice_in_dim(down_weight, me * owned_rows, owned_rows, 0).astype(
        jnp.float32
    )
    new_shard = (
        old_shard
        - learn_rate
        * (corrected_one / (jnp.sqrt(corrected_two) + epsilon) + decay_rate * old_shard)
    ).astype(jnp.bfloat16)
    partial_out = lax.dot_general(
        new_shard, next_all, (((1,), (1,)), ((), ())), preferred_element_type=jnp.float32
    )
    summed = (
        lax.psum_scatter(partial_out, "tensor", scatter_dimension=1, tiled=True)
        .astype(jnp.bfloat16)
        .T
    )
    sub = me % group
    pieces = []
    for k in range(group):
        s = (sub + k) % group
        piece = lax.dynamic_slice_in_dim(summed, s * tok, tok, 0)
        perm = []
        for i in range(n_dp):
            for j in range(n_t):
                si = (i % group + k) % group
                dst = (group * j + si) * n_t + i // group
                perm.append((i * n_t + j, dst))
        pieces.append(lax.ppermute(piece, ("dp", "tensor"), perm))
    ordered = []
    for r in range(group):
        chosen = pieces[0]
        for k in range(1, group):
            chosen = jnp.where((sub - k) % group == r, pieces[k], chosen)
        ordered.append(chosen)
    next_out = jnp.concatenate(ordered, axis=1)
    return (gate_grad, up_grad, moment_one, moment_two, next_out)


def solution(mesh):
    n_dp = mesh.shape["dp"]
    n_t = mesh.shape["tensor"]
    if n_dp % n_t:
        raise ValueError("bad mesh")
    placed = (
        P("dp", None),
        P("dp", "tensor"),
        P("dp", "tensor"),
        P("dp", "tensor"),
        P(None, "tensor"),
        P("dp", "tensor"),
        P("dp", "tensor"),
    )
    return jax.shard_map(
        shards,
        mesh=mesh,
        in_specs=placed,
        out_specs=(
            P("dp", "tensor"),
            P("dp", "tensor"),
            P("dp", "tensor"),
            P("dp", "tensor"),
            P("dp", "tensor"),
        ),
        check_vma=False,
    )
```

profile of v0, /device:TPU:3, one launch (start us, length us, event | category | flops | bytes accessed | tf_op | source)
XLA Modules:
  0.0 363.5 jit_solution(1253085345670090751)
XLA Ops:
  7.2 21.4 %multiply_convert_fusion = (bf16[256,3584]{1,0:T(8,128)(2,1)}, bf16[256,3584]{1,0:T(8,128)(2,1)}, bf16[256,3584]{1,0:T(8,128)(2,1)}) fusion(bf16[256,3584]{1,0:T(8,128)(2,1)} %param.8, bf16[256,3584]{1,0:T(8,128)(2,1)} %param.9, bf16[256,4096]{1,0:T(8,128)(2,1)} %param.7, bf16[4096,3584]{1,0:T(8,128)(2,1)} %param.11), kind=kOutput, calls=%fused_computation.31 | convolution fusion | flops 7531790336 | bytes 40632320 | tf_op jit(solution)/shard_map/dot_general | solution.py:30
  28.6 0.0 all-gather.5.cloned.1.call-start
  28.6 0.7 all-gather.5.cloned.1.call-update
  29.3 0.8 copy-done.1
  30.2 2.5 copy.25
  32.7 4.6 %all-to-all-start = ((bf16[8,512,256]{2,1,0:T(8,128)(2,1)}), bf16[8,512,256]{2,1,0:T(8,128)(2,1)S(1)}, u32[]{:S(2)}, u32[]{:S(2)}) async-start(bf16[8,512,256]{2,1,0:T(8,128)(2,1)} %bitcast.18), calls=%async_computation | async-start | bytes 4194304 | tf_op jit(solution)/shard_map/all_to_all | solution.py:29
  37.2 8.9 %copy.27 = f32[512,3584]{0,1:T(8,128)} copy(f32[512,3584]{1,0:T(8,128)} %param.13) | data formatting | bytes 14680064 | tf_op args[6]
  46.1 8.4 %copy.24 = f32[512,3584]{0,1:T(8,128)} copy(f32[512,3584]{1,0:T(8,128)} %param.12) | data formatting | bytes 14680064 | tf_op args[5]
  54.5 4.1 %constant_dynamic-slice_fusion = bf16[512,3584]{1,0:T(8,128)(2,1)} fusion(bf16[4096,3584]{1,0:T(8,128)(2,1)} %param.11, s32[]{:T(128)S(6)} %select_n.47), kind=kLoop, calls=%fused_computation.54 | loop fusion | bytes 7340036 | tf_op jit(solution)/shard_map/dynamic_slice | solution.py:47
  58.5 6.0 %copy.32 = bf16[512,3584]{0,1:T(8,128)(2,1)} copy(bf16[512,3584]{1,0:T(8,128)(2,1)} %constant_dynamic-slice_fusion) | data formatting | bytes 7340032
  64.5 15.2 %all-to-all-done = bf16[8,512,256]{2,1,0:T(8,128)(2,1)S(1)} async-done(((bf16[8,512,256]{2,1,0:T(8,128)(2,1)}), bf16[8,512,256]{2,1,0:T(8,128)(2,1)S(1)}, u32[]{:S(2)}, u32[]{:S(2)}) %all-to-all-start) | async-done | bytes 2097184 | tf_op jit(solution)/shard_map/all_to_all | solution.py:29
  79.7 2.4 copy.26
  82.1 49.7 %all-gather.3.cloned.1.call-done = bf16[2048,3584]{1,0:T(8,128)(2,1)} async-done(((bf16[256,3584]{1,0:T(8,128)(2,1)}), bf16[2048,3584]{1,0:T(8,128)(2,1)}) %all-gather.3.cloned.1.call-update) | async-done | bytes 14680080 | tf_op jit(solution)/shard_map/all_gather | solution.py:27
  131.8 4.7 %convolution_convert_fusion = bf16[3584,512]{1,0:T(8,128)(2,1)} fusion(bf16[2048,3584]{1,0:T(8,128)(2,1)} %all-gather.3.cloned.1.call-done, bf16[512,2048]{0,1:T(8,128)(2,1)} %bitcast.19), kind=kOutput, calls=%fused_computation.10 | convolution fusion | flops 941359104 | bytes 5767168 | tf_op jit(solution)/shard_map/dot_general | solution.py:37
  136.5 5.3 %convolution_convert_fusion.1 = bf16[3584,512]{1,0:T(8,128)(2,1)} fusion(bf16[2048,3584]{1,0:T(8,128)(2,1)} %all-gather.3.cloned.1.call-done, bf16[512,2048]{0,1:T(8,128)(2,1)S(1)} %bitcast.20), kind=kOutput, calls=%fused_computation.11 | convolution fusion | flops 941359104 | bytes 5767168 | tf_op jit(solution)/shard_map/dot_general | solution.py:37
  141.8 2.9 convolution_convert_fusion.2
  144.8 3.1 convolution_convert_fusion.3
  147.8 3.0 convolution_convert_fusion.4
  150.8 2.9 convolution_convert_fusion.5
  153.8 3.0 convolution_convert_fusion.6
  156.7 20.0 %fusion.3 = (f32[512,3584]{0,1:T(8,128)}, f32[512,3584]{0,1:T(8,128)}) fusion(f32[512,3584]{0,1:T(8,128)} %copy.27, f32[512,3584]{0,1:T(8,128)} %copy.24, bf16[3584,512]{1,0:T(8,128)(2,1)} %convolution_convert_fusion, bf16[3584,512]{1,0:T(8,128)(2,1)} %convolution_convert_fusion.1, bf16[3584,512]{1,0:T(8,128)(2,1)} %convolution_convert_fusion.2, ...), kind=kOutput, calls=%fused_computation.6 | convolution fusion | flops 981729280 | bytes 57147392 | tf_op jit(solution)/shard_map/dot_general | solution.py:37
  176.8 38.0 %all-gather.5.cloned.1.call-done = bf16[2048,3584]{1,0:T(8,128)(2,1)} async-done(((bf16[256,3584]{1,0:T(8,128)(2,1)}), bf16[2048,3584]{1,0:T(8,128)(2,1)}) %all-gather.5.cloned.1.call-update) | async-done | bytes 14680080 | tf_op jit(solution)/shard_map/all_gather | solution.py:28
  214.7 25.4 %fusion.13 = f32[512,2048]{1,0:T(8,128)} fusion(bf16[2048,3584]{1,0:T(8,128)(2,1)} %all-gather.5.cloned.1.call-done, bf16[512,3584]{0,1:T(8,128)(2,1)} %copy.32, f32[512,3584]{0,1:T(8,128)} %get-tuple-element.20, f32[512,3584]{0,1:T(8,128)} %get-tuple-element.21), kind=kOutput, calls=%fused_computation.32 | convolution fusion | flops 7534542848 | bytes 37224448 | tf_op jit(solution)/shard_map/dot_general | solution.py:55
  240.2 76.5 %reduce-scatter.2.cloned.1.call-done = f32[512,512]{1,0:T(8,128)} async-done(((f32[512,2048]{1,0:T(8,128)}), f32[512,512]{1,0:T(8,128)}) %reduce-scatter.2.cloned.1.call-update) | async-done | bytes 1048592 | tf_op jit(solution)/shard_map/reduce_scatter | solution.py:59
  316.7 1.3 convert_element_type.126
  318.0 1.8 collective-permute-start
  319.8 3.1 collective-permute-start.1
  322.9 8.4 %copy.29 = f32[512,3584]{1,0:T(8,128)} copy(f32[512,3584]{0,1:T(8,128)} %get-tuple-element.21) | data formatting | bytes 14680064
  331.3 8.4 %copy.30 = f32[512,3584]{1,0:T(8,128)} copy(f32[512,3584]{0,1:T(8,128)} %get-tuple-element.20) | data formatting | bytes 14680064
  339.6 10.6 %collective-permute-done = bf16[256,512]{0,1:T(8,128)(2,1)S(1)} collective-permute-done((bf16[256,512]{0,1:T(8,128)(2,1)S(1)}, bf16[256,512]{0,1:T(8,128)(2,1)S(1)}, u32[]{:S(2)}, u32[]{:S(2)}) %collective-permute-start) | collective-permute-done | bytes 262176 | tf_op jit(solution)/shard_map/ppermute | solution.py:74
  350.2 5.6 %collective-permute-done.1 = bf16[256,512]{0,1:T(8,128)(2,1)S(1)} collective-permute-done((bf16[256,512]{0,1:T(8,128)(2,1)S(1)}, bf16[256,512]{0,1:T(8,128)(2,1)S(1)}, u32[]{:S(2)}, u32[]{:S(2)}) %collective-permute-start.1) | collective-permute-done | bytes 262176 | tf_op jit(solution)/shard_map/ppermute | solution.py:74
  355.9 1.0 copy.31
  (12 shorter events, 0.2 us)
Async XLA Ops:
  7.2 124.7 %all-gather.3.cloned.1.call-start = ((), (), s32[]{:S(2)}) async-start(), calls=%async_computation.2 | async-start | bytes 16515072 | tf_op jit(solution)/shard_map/all_gather | solution.py:27
  28.6 1.6 copy-start.1
  28.6 186.1 %all-gather.5.cloned.1.call-start = ((), (), s32[]{:S(2)}) async-start(), calls=%async_computation.3 | async-start | bytes 16515072 | tf_op jit(solution)/shard_map/all_gather | solution.py:28
  32.7 47.1 %all-to-all-start = ((bf16[8,512,256]{2,1,0:T(8,128)(2,1)}), bf16[8,512,256]{2,1,0:T(8,128)(2,1)S(1)}, u32[]{:S(2)}, u32[]{:S(2)}) async-start(bf16[8,512,256]{2,1,0:T(8,128)(2,1)} %bitcast.18), calls=%async_computation | async-start | bytes 4194304 | tf_op jit(solution)/shard_map/all_to_all | solution.py:29
  37.2 279.4 %reduce-scatter.2.cloned.1.call-start = ((), (), s32[]{:S(2)}) async-start(), calls=%async_computation.4 | async-start | bytes 5242880 | tf_op jit(solution)/shard_map/reduce_scatter | solution.py:59
  131.8 4.7 %copy-start = (bf16[512,8,256]{0,2,1:T(8,128)(2,1)S(1)}, bf16[512,8,256]{0,2,1:T(8,128)(2,1)}, u32[]{:S(2)}) copy-start(bf16[512,8,256]{0,2,1:T(8,128)(2,1)} %copy.26) | copy-start | bytes 6291460
  131.8 10.0 %copy-start.2 = (bf16[2048,3584]{1,0:T(8,128)(2,1)S(1)}, bf16[2048,3584]{1,0:T(8,128)(2,1)}, u32[]{:S(2)}) copy-start(bf16[2048,3584]{1,0:T(8,128)(2,1)} %all-gather.3.cloned.1.call-done) | copy-start | bytes 44040196
  318.0 32.2 %collective-permute-start = (bf16[256,512]{0,1:T(8,128)(2,1)S(1)}, bf16[256,512]{0,1:T(8,128)(2,1)S(1)}, u32[]{:S(2)}, u32[]{:S(2)}) collective-permute-start(bf16[256,512]{0,1:T(8,128)(2,1)S(1)} %get-tuple-element.28), channel_id=1, source_target_pairs={{0,4},{1,12},{2,20},{3,28},{4,0},{5,8},{6,16},{7,24},{8,5},{9,13},... | collective-permute-start | bytes 786440 | tf_op jit(solution)/shard_map/ppermute | solution.py:74
  319.8 36.1 %collective-permute-start.1 = (bf16[256,512]{0,1:T(8,128)(2,1)S(1)}, bf16[256,512]{0,1:T(8,128)(2,1)S(1)}, u32[]{:S(2)}, u32[]{:S(2)}) collective-permute-start(bf16[256,512]{0,1:T(8,128)(2,1)S(1)} %get-tuple-element.27), channel_id=1, source_target_pairs={{0,0},{1,8},{2,16},{3,24},{4,4},{5,12},{6,20},{7,28},{8,1},{9,9},{... | collective-permute-start | bytes 786440 | tf_op jit(solution)/shard_map/ppermute | solution.py:74
Sparse Core Ops, SparseCore 0:
  28.7 103.0 all-gather.2
  133.7 80.9 all-gather.4
  240.2 76.3 reduce-scatter.1
where the time goes:
time: 364 us; the launch traced here: 363 us
  waiting for transfers between devices  196 us (54%)
  matrix products  91.7 us (25%)
  local copies, waits for them, and re-layouts  50.8 us (14%)
  between operations  13.8 us (4%)
  starting transfers between devices  9.51 us (3%)
    reduce_scatter x1, waiting for transfers between devices, shards(): lax.psum_scatter(partial_out, 'tensor', scatter_dimension=1, tiled=True)  76.5 us
    all_gather x1, waiting for transfers between devices, shards(): hidden_all = lax.all_gather(hidden, 'dp', axis=0, tiled=True)  49.7 us
    dot_general x8, matrix products, shards(): jnp.dot(grad_rows[:, b * tok:(b + 1) * tok], hidden_all[b * tok:(b + 1) *...  44.9 us
    unnamed x13, local copies, waits for them, and re-layouts  44.3 us
    all_gather x1, waiting for transfers between devices, shards(): next_all = lax.all_gather(next_hidden, 'dp', axis=0, tiled=True)  38 us
    dot_general x1, matrix products, shards(): lax.dot_general(new_shard, next_all, (((1,), (1,)), ((), ())), preferred_...  25.4 us
    dot_general x1, matrix products, shards(): jnp.dot(grad_out, down_weight, preferred_element_type=jnp.float32)  21.4 us
    ppermute x2, waiting for transfers between devices, shards(): pieces.append(lax.ppermute(piece, ('dp', 'tensor'), perm))  16.2 us
  transfers between devices with their start and end apart: 6, of which 6 were waited for; matrix products, arithmetic and copies ran while one was open for 26% of the time, Pallas kernels for 0%

commit v1 on v0

--- a/solution.py
+++ b/solution.py
@@ -9,6 +9,27 @@
 learn_rate = 0.001
 decay_rate = 0.1
 epsilon = 1e-08
+
+
+def gather_around(x, axis, dim):
+    size, index, extent = (lax.axis_size(axis), lax.axis_index(axis), x.shape[dim])
+    right = [(i, (i + 1) % size) for i in range(size)]
+    left = [(i, (i - 1) % size) for i in range(size)]
+    out = jnp.zeros((*x.shape[:dim], size * extent, *x.shape[dim + 1 :]), x.dtype)
+    out = lax.dynamic_update_slice_in_dim(out, x, index * extent, axis=dim)
+    from_left = from_right = x
+    middle = size // 2
+    for step in range(1, middle + 1):
+        from_left = lax.ppermute(from_left, axis, right)
+        out = lax.dynamic_update_slice_in_dim(
+            out, from_left, (index - step) % size * extent, axis=dim
+        )
+        if step < size - middle:
+            from_right = lax.ppermute(from_right, axis, left)
+            out = lax.dynamic_update_slice_in_dim(
+                out, from_right, (index + step) % size * extent, axis=dim
+            )
+    return out
 
 
 def shards(grad_out, gate_input, up_input, next_hidden, down_weight, first_moment, second_moment):
@@ -25,7 +46,7 @@
     activated = gate_value * sigmoid_gate
     hidden = (activated * up_value).astype(jnp.bfloat16)
     hidden_all = lax.all_gather(hidden, "dp", axis=0, tiled=True)
-    next_all = lax.all_gather(next_hidden, "dp", axis=0, tiled=True)
+    next_all = gather_around(next_hidden, "dp", 0)
     grad_rows = lax.all_to_all(grad_out.T, "dp", 0, 1, tiled=True)
     grad_hidden = jnp.dot(grad_out, down_weight, preferred_element_type=jnp.float32)
     gate_grad = (

time: 364 us -> 448 us (1.23)
  waiting for transfers between devices: 196 us -> 244 us
  local copies, waits for them, and re-layouts: 50.8 us -> 75.9 us
  starting transfers between devices: 9.51 us -> 20.5 us
    ppermute x0 -> x7, waiting for transfers between devices: none -> 149 us  [the longest x4 148 us: gather_around(): from_left = lax.ppermute(from_left, axis, right)]
    all_gather x1, waiting for transfers between devices: 49.7 us -> 0.01 us  [shards(): hidden_all = lax.all_gather(hidden, 'dp', axis=0, tiled=True)]
    all_gather x1 -> x0, waiting for transfers between devices: 38 us -> none  [shards(): next_all = lax.all_gather(next_hidden, 'dp', axis=0, tiled=True)]
    dynamic_update_slice x0 -> x8, local copies, waits for them, and re-layouts: none -> 20.1 us  [the longest x4 9.96 us: gather_around(): lax.dynamic_update_slice_in_dim(out, from_left, (index - step) % size * e...]
    all_to_all x1, waiting for transfers between devices: 15.2 us -> 0.1 us  [shards(): grad_rows = lax.all_to_all(grad_out.T, 'dp', 0, 1, tiled=True)]
    ppermute x0 -> x7, starting transfers between devices: none -> 12 us  [the longest x4 12 us: gather_around(): from_left = lax.ppermute(from_left, axis, right)]
    broadcast_in_dim x0 -> x1, local copies, waits for them, and re-layouts: none -> 6.11 us  [gather_around(): jnp.zeros((*x.shape[:dim], size * extent, *x.shape[dim + 1:]), x.dtype)]
  transfers between devices with their start and end apart: 6 -> 12, of which waited for: 6 -> 9; matrix products, arithmetic and copies ran while one was open for 26% -> 17% of each run, Pallas kernels for 0% -> 0%
where the time goes in v1:
time: 448 us
  waiting for transfers between devices  244 us (54%)
  matrix products  91.3 us (20%)
  local copies, waits for them, and re-layouts  75.9 us (17%)
  starting transfers between devices  20.5 us (5%)
  between operations  14.3 us (3%)
    ppermute x4, waiting for transfers between devices, gather_around(): from_left = lax.ppermute(from_left, axis, right)  148 us
    reduce_scatter x1, waiting for transfers between devices, shards(): lax.psum_scatter(partial_out, 'tensor', scatter_dimension=1, tiled=True)  78.7 us
    dot_general x8, matrix products, shards(): jnp.dot(grad_rows[:, b * tok:(b + 1) * tok], hidden_all[b * tok:(b + 1) *...  44.4 us
    unnamed x13, local copies, waits for them, and re-layouts  43.1 us
    dot_general x1, matrix products, shards(): lax.dot_general(new_shard, next_all, (((1,), (1,)), ((), ())), preferred_...  25.5 us
    dot_general x1, matrix products, shards(): jnp.dot(grad_out, down_weight, preferred_element_type=jnp.float32)  21.4 us
    ppermute x2, waiting for transfers between devices, shards(): pieces.append(lax.ppermute(piece, ('dp', 'tensor'), perm))  16.2 us
    ppermute x4, starting transfers between devices, gather_around(): from_left = lax.ppermute(from_left, axis, right)  12 us
  transfers between devices with their start and end apart: 12, of which 9 were waited for; matrix products, arithmetic and copies ran while one was open for 17% of the time, Pallas kernels for 0%

profile of v1, /device:TPU:3, one launch (start us, length us, event | category | flops | bytes accessed | tf_op | source)
XLA Modules:
  0.0 447.5 jit_solution(9434962720021613267)
XLA Ops:
  7.2 21.4 %multiply_convert_fusion = (bf16[256,3584]{1,0:T(8,128)(2,1)}, bf16[256,3584]{1,0:T(8,128)(2,1)}, bf16[256,3584]{1,0:T(8,128)(2,1)}) fusion(bf16[256,3584]{1,0:T(8,128)(2,1)} %param.8, bf16[256,3584]{1,0:T(8,128)(2,1)} %param.9, bf16[256,4096]{1,0:T(8,128)(2,1)} %param.7, bf16[4096,3584]{1,0:T(8,128)(2,1)} %param.11), kind=kOutput, calls=%fused_computation.31 | convolution fusion | flops 7531790336 | bytes 40632320 | tf_op jit(solution)/shard_map/dot_general | solution.py:51
  30.5 61.3 %collective-permute-done = bf16[256,3584]{1,0:T(8,128)(2,1)} collective-permute-done((bf16[256,3584]{1,0:T(8,128)(2,1)}, bf16[256,3584]{1,0:T(8,128)(2,1)}, u32[]{:S(2)}, u32[]{:S(2)}) %collective-permute-start) | collective-permute-done | bytes 1835040 | tf_op jit(solution)/shard_map/ppermute | solution.py:23
  91.8 3.4 collective-permute-start.2
  97.7 3.6 all-to-all-start
  101.5 8.5 %copy.27 = f32[512,3584]{0,1:T(8,128)} copy(f32[512,3584]{1,0:T(8,128)} %param.13) | data formatting | bytes 14680064 | tf_op args[6]
  110.0 8.4 %copy.24 = f32[512,3584]{0,1:T(8,128)} copy(f32[512,3584]{1,0:T(8,128)} %param.12) | data formatting | bytes 14680064 | tf_op args[5]
  118.4 48.5 %collective-permute-done.2 = bf16[256,3584]{1,0:T(8,128)(2,1)} collective-permute-done((bf16[256,3584]{1,0:T(8,128)(2,1)}, bf16[256,3584]{1,0:T(8,128)(2,1)}, u32[]{:S(2)}, u32[]{:S(2)}) %collective-permute-start.2) | collective-permute-done | bytes 1835040 | tf_op jit(solution)/shard_map/ppermute | solution.py:23
  166.9 3.4 collective-permute-start.4
  170.3 4.1 constant_dynamic-slice_fusion
  174.4 5.9 %copy.32 = bf16[512,3584]{0,1:T(8,128)(2,1)} copy(bf16[512,3584]{1,0:T(8,128)(2,1)} %constant_dynamic-slice_fusion) | data formatting | bytes 7340032
  180.3 6.1 %broadcast_in_dim.3 = bf16[2048,3584]{1,0:T(8,128)(2,1)} broadcast(bf16[]{:T(256)} %constant.102.clone.1), dimensions={} | broadcast | bytes 14680066 | tf_op jit(solution)/shard_map/broadcast_in_dim | solution.py:18
  195.8 2.9 constant_dynamic-update-slice_fusion.5
  198.7 26.3 %collective-permute-done.4 = bf16[256,3584]{1,0:T(8,128)(2,1)} collective-permute-done((bf16[256,3584]{1,0:T(8,128)(2,1)}, bf16[256,3584]{1,0:T(8,128)(2,1)}, u32[]{:S(2)}, u32[]{:S(2)}) %collective-permute-start.4) | collective-permute-done | bytes 1835040 | tf_op jit(solution)/shard_map/ppermute | solution.py:23
  225.0 3.4 collective-permute-start.6
  228.4 2.9 constant_dynamic-update-slice_fusion.4
  231.3 3.1 constant_dynamic-update-slice_fusion.3
  238.6 11.8 %collective-permute-done.6 = bf16[256,3584]{1,0:T(8,128)(2,1)S(1)} collective-permute-done((bf16[256,3584]{1,0:T(8,128)(2,1)}, bf16[256,3584]{1,0:T(8,128)(2,1)S(1)}, u32[]{:S(2)}, u32[]{:S(2)}) %collective-permute-start.6) | collective-permute-done | bytes 1835040 | tf_op jit(solution)/shard_map/ppermute | solution.py:23
  251.8 4.7 %convolution_convert_fusion = bf16[3584,512]{1,0:T(8,128)(2,1)} fusion(bf16[2048,3584]{1,0:T(8,128)(2,1)} %all-gather.2.cloned.1.call-done, bf16[512,2048]{0,1:T(8,128)(2,1)S(1)} %bitcast.19), kind=kOutput, calls=%fused_computation.10 | convolution fusion | flops 941359104 | bytes 5767168 | tf_op jit(solution)/shard_map/dot_general | solution.py:58
  256.5 5.3 %convolution_convert_fusion.1 = bf16[3584,512]{1,0:T(8,128)(2,1)} fusion(bf16[2048,3584]{1,0:T(8,128)(2,1)} %all-gather.2.cloned.1.call-done, bf16[512,2048]{0,1:T(8,128)(2,1)S(1)} %bitcast.20), kind=kOutput, calls=%fused_computation.11 | convolution fusion | flops 941359104 | bytes 5767168 | tf_op jit(solution)/shard_map/dot_general | solution.py:58
  261.8 2.9 convolution_convert_fusion.2
  264.7 3.1 convolution_convert_fusion.3
  267.8 3.0 convolution_convert_fusion.4
  270.8 3.0 convolution_convert_fusion.5
  273.7 3.0 convolution_convert_fusion.6
  276.7 19.4 %fusion.3 = (f32[512,3584]{0,1:T(8,128)}, f32[512,3584]{0,1:T(8,128)}) fusion(f32[512,3584]{0,1:T(8,128)} %copy.27, f32[512,3584]{0,1:T(8,128)} %copy.24, bf16[3584,512]{1,0:T(8,128)(2,1)} %convolution_convert_fusion, bf16[3584,512]{1,0:T(8,128)(2,1)} %convolution_convert_fusion.1, bf16[3584,512]{1,0:T(8,128)(2,1)} %convolution_convert_fusion.2, ...), kind=kOutput, calls=%fused_computation.6 | convolution fusion | flops 981729280 | bytes 57147392 | tf_op jit(solution)/shard_map/dot_general | solution.py:58
  296.1 25.5 %fusion.13 = f32[512,2048]{1,0:T(8,128)} fusion(bf16[2048,3584]{1,0:T(8,128)(2,1)} %constant_dynamic-update-slice_fusion, bf16[512,3584]{0,1:T(8,128)(2,1)} %copy.32, f32[512,3584]{0,1:T(8,128)} %get-tuple-element.20, f32[512,3584]{0,1:T(8,128)} %get-tuple-element.21), kind=kOutput, calls=%fused_computation.32 | convolution fusion | flops 7534542848 | bytes 37224448 | tf_op jit(solution)/shard_map/dot_general | solution.py:76
  321.7 78.7 %reduce-scatter.2.cloned.1.call-done = f32[512,512]{1,0:T(8,128)} async-done(((f32[512,2048]{1,0:T(8,128)}), f32[512,512]{1,0:T(8,128)}) %reduce-scatter.2.cloned.1.call-update) | async-done | bytes 1048592 | tf_op jit(solution)/shard_map/reduce_scatter | solution.py:80
  403.6 3.0 collective-permute-start.8
  406.7 8.4 %copy.29 = f32[512,3584]{1,0:T(8,128)} copy(f32[512,3584]{0,1:T(8,128)} %get-tuple-element.21) | data formatting | bytes 14680064
  415.0 8.4 %copy.30 = f32[512,3584]{1,0:T(8,128)} copy(f32[512,3584]{0,1:T(8,128)} %get-tuple-element.20) | data formatting | bytes 14680064
  423.4 10.6 %collective-permute-done.7 = bf16[256,512]{0,1:T(8,128)(2,1)S(1)} collective-permute-done((bf16[256,512]{0,1:T(8,128)(2,1)S(1)}, bf16[256,512]{0,1:T(8,128)(2,1)S(1)}, u32[]{:S(2)}, u32[]{:S(2)}) %collective-permute-start.7) | collective-permute-done | bytes 262176 | tf_op jit(solution)/shard_map/ppermute | solution.py:95
  434.0 5.6 %collective-permute-done.8 = bf16[256,512]{0,1:T(8,128)(2,1)S(1)} collective-permute-done((bf16[256,512]{0,1:T(8,128)(2,1)S(1)}, bf16[256,512]{0,1:T(8,128)(2,1)S(1)}, u32[]{:S(2)}, u32[]{:S(2)}) %collective-permute-start.8) | collective-permute-done | bytes 262176 | tf_op jit(solution)/shard_map/ppermute | solution.py:95
  (32 shorter events, 23.7 us)
Async XLA Ops:
  7.2 88.0 %copy-start.1 = (bf16[256,4096]{1,0:T(8,128)(2,1)S(1)}, bf16[256,4096]{1,0:T(8,128)(2,1)}, u32[]{:S(2)}) copy-start(bf16[256,4096]{1,0:T(8,128)(2,1)} %param.7) | copy-start | bytes 6291460
  7.2 244.6 %all-gather.2.cloned.1.call-start = ((), (), s32[]{:S(2)}) async-start(), calls=%async_computation.2 | async-start | bytes 16515072 | tf_op jit(solution)/shard_map/all_gather | solution.py:48
  28.7 63.1 %collective-permute-start = (bf16[256,3584]{1,0:T(8,128)(2,1)}, bf16[256,3584]{1,0:T(8,128)(2,1)}, u32[]{:S(2)}, u32[]{:S(2)}) collective-permute-start(bf16[256,3584]{1,0:T(8,128)(2,1)} %param.10), channel_id=1, source_target_pairs={{0,4},{4,8},{8,12},{12,16},{16,20},{20,24},{24,28},{28,0},{1,5},{5... | collective-permute-start | bytes 5505032 | tf_op jit(solution)/shard_map/ppermute | solution.py:23
  30.5 70.8 %collective-permute-start.1 = (bf16[256,3584]{1,0:T(8,128)(2,1)}, bf16[256,3584]{1,0:T(8,128)(2,1)}, u32[]{:S(2)}, u32[]{:S(2)}) collective-permute-start(bf16[256,3584]{1,0:T(8,128)(2,1)} %param.10), channel_id=1, source_target_pairs={{0,28},{4,0},{8,4},{12,8},{16,12},{20,16},{24,20},{28,24},{1,29},{... | collective-permute-start | bytes 5505032 | tf_op jit(solution)/shard_map/ppermute | solution.py:28
  91.8 75.1 %collective-permute-start.2 = (bf16[256,3584]{1,0:T(8,128)(2,1)}, bf16[256,3584]{1,0:T(8,128)(2,1)}, u32[]{:S(2)}, u32[]{:S(2)}) collective-permute-start(bf16[256,3584]{1,0:T(8,128)(2,1)} %collective-permute-done), channel_id=1, source_target_pairs={{0,4},{4,8},{8,12},{12,16},{16,20},{20,24},{24,28},{28,0},{1,5},{5... | collective-permute-start | bytes 5505032 | tf_op jit(solution)/shard_map/ppermute | solution.py:23
  97.7 91.7 %all-to-all-start = ((bf16[8,512,256]{2,1,0:T(8,128)(2,1)}), bf16[8,512,256]{2,1,0:T(8,128)(2,1)S(1)}, u32[]{:S(2)}, u32[]{:S(2)}) async-start(bf16[8,512,256]{2,1,0:T(8,128)(2,1)} %bitcast.18), calls=%async_computation | async-start | bytes 4194304 | tf_op jit(solution)/shard_map/all_to_all | solution.py:50
  101.3 299.2 %reduce-scatter.2.cloned.1.call-start = ((), (), s32[]{:S(2)}) async-start(), calls=%async_computation.3 | async-start | bytes 5242880 | tf_op jit(solution)/shard_map/reduce_scatter | solution.py:80
  101.3 94.5 %collective-permute-start.3 = (bf16[256,3584]{1,0:T(8,128)(2,1)}, bf16[256,3584]{1,0:T(8,128)(2,1)}, u32[]{:S(2)}, u32[]{:S(2)}) collective-permute-start(bf16[256,3584]{1,0:T(8,128)(2,1)} %collective-permute-done.1), channel_id=1, source_target_pairs={{0,28},{4,0},{8,4},{12,8},{16,12},{20,16},{24,20},{28,24},{1,29},{... | collective-permute-start | bytes 5505032 | tf_op jit(solution)/shard_map/ppermute | solution.py:28
  166.9 58.1 %collective-permute-start.4 = (bf16[256,3584]{1,0:T(8,128)(2,1)}, bf16[256,3584]{1,0:T(8,128)(2,1)}, u32[]{:S(2)}, u32[]{:S(2)}) collective-permute-start(bf16[256,3584]{1,0:T(8,128)(2,1)} %collective-permute-done.2), channel_id=1, source_target_pairs={{0,4},{4,8},{8,12},{12,16},{16,20},{20,24},{24,28},{28,0},{1,5},{5... | collective-permute-start | bytes 5505032 | tf_op jit(solution)/shard_map/ppermute | solution.py:23
  195.8 41.4 %collective-permute-start.5 = (bf16[256,3584]{1,0:T(8,128)(2,1)}, bf16[256,3584]{1,0:T(8,128)(2,1)S(1)}, u32[]{:S(2)}, u32[]{:S(2)}) collective-permute-start(bf16[256,3584]{1,0:T(8,128)(2,1)} %collective-permute-done.3), channel_id=1, source_target_pairs={{0,28},{4,0},{8,4},{12,8},{16,12},{20,16},{24,20},{28,24},{1,29},{... | collective-permute-start | bytes 5505032 | tf_op jit(solution)/shard_map/ppermute | solution.py:28
  225.0 25.4 %collective-permute-start.6 = (bf16[256,3584]{1,0:T(8,128)(2,1)}, bf16[256,3584]{1,0:T(8,128)(2,1)S(1)}, u32[]{:S(2)}, u32[]{:S(2)}) collective-permute-start(bf16[256,3584]{1,0:T(8,128)(2,1)} %collective-permute-done.4), channel_id=1, source_target_pairs={{0,4},{4,8},{8,12},{12,16},{16,20},{20,24},{24,28},{28,0},{1,5},{5... | collective-permute-start | bytes 5505032 | tf_op jit(solution)/shard_map/ppermute | solution.py:23
  231.3 20.5 %copy-start = (bf16[512,8,256]{0,2,1:T(8,128)(2,1)S(1)}, bf16[512,8,256]{0,2,1:T(8,128)(2,1)}, u32[]{:S(2)}) copy-start(bf16[512,8,256]{0,2,1:T(8,128)(2,1)} %copy.26) | copy-start | bytes 6291460
  251.8 10.0 %copy-start.2 = (bf16[2048,3584]{1,0:T(8,128)(2,1)S(1)}, bf16[2048,3584]{1,0:T(8,128)(2,1)}, u32[]{:S(2)}) copy-start(bf16[2048,3584]{1,0:T(8,128)(2,1)} %all-gather.2.cloned.1.call-done) | copy-start | bytes 44040196
  401.8 32.2 %collective-permute-start.7 = (bf16[256,512]{0,1:T(8,128)(2,1)S(1)}, bf16[256,512]{0,1:T(8,128)(2,1)S(1)}, u32[]{:S(2)}, u32[]{:S(2)}) collective-permute-start(bf16[256,512]{0,1:T(8,128)(2,1)S(1)} %get-tuple-element.28), channel_id=1, source_target_pairs={{0,4},{1,12},{2,20},{3,28},{4,0},{5,8},{6,16},{7,24},{8,5},{9,13},... | collective-permute-start | bytes 786440 | tf_op jit(solution)/shard_map/ppermute | solution.py:95
  403.6 36.0 %collective-permute-start.8 = (bf16[256,512]{0,1:T(8,128)(2,1)S(1)}, bf16[256,512]{0,1:T(8,128)(2,1)S(1)}, u32[]{:S(2)}, u32[]{:S(2)}) collective-permute-start(bf16[256,512]{0,1:T(8,128)(2,1)S(1)} %get-tuple-element.27), channel_id=1, source_target_pairs={{0,0},{1,8},{2,16},{3,24},{4,4},{5,12},{6,20},{7,28},{8,1},{9,9},{... | collective-permute-start | bytes 786440 | tf_op jit(solution)/shard_map/ppermute | solution.py:95
Sparse Core Ops, SparseCore 0:
  28.8 136.1 all-gather.1
  321.8 78.6 reduce-scatter.1
